TPU v7x, 256 devices: a whole 4x4x8 slice. The times are simulated.
256 devices in a mesh: gx: 8 (over z), gy: 32 (over y, x, core).
Axes of the slice: x: 4, y: 4, z: 8, core: 2. Of those that a mesh axis runs over, the one named last changes fastest.
Arguments:
- saved_pops: bfloat16 [4, 19, 128, 16384], P(None, None, 'gx', 'gy'), may hold values from 0.099609375 to 1.8984375
- seed_adjoint: float32 [19, 128, 16384], P(None, 'gx', 'gy'), may hold values from -6 to 6
- solid_label: int32 [128, 16384], P('gx', 'gy'), may hold values 0 or 1
- design_mask: int32 [128, 16384], P('gx', 'gy'), may hold values 0 or 1
- design_field: float32 [128, 16384], P('gx', 'gy'), may hold values from 0 to 1
Outputs:
- adjoint_out: float32 [19, 128, 16384], P(None, 'gx', 'gy')
- sensitivity: float32 [128, 16384], P('gx', 'gy')
All inputs are finite; a program needn't handle non-finite values. No bound on the sum of `solid_label` or of `design_mask` on one device may be relied on, other than what follows from the above.
Results may differ from a plain program's by a relative error of at most 0.0003.
Values sent between devices are 32-bit elements; how exact they have to be, the bound alone decides.
No kernel may reach another device: no remote copies, remote signals or barrier semaphores. Data moves between devices by JAX's collectives and lax.ppermute only.
A program may use at most 64 MiB of HBM per device.

v0:
```python
import jax
import jax.numpy as jnp
import numpy as np
from jax import lax
from jax.experimental import pallas as pl
from jax.experimental.pallas import tpu as pltpu
from jax.sharding import PartitionSpec as P

NZ = 32


VELOCITIES = np.array(
    [
        [0, 0, 0],
        [1, 0, 0],
        [-1, 0, 0],
        [0, 1, 0],
        [0, -1, 0],
        [0, 0, 1],
        [0, 0, -1],
        [1, 1, 0],
        [1, -1, 0],
        [-1, 1, 0],
        [-1, -1, 0],
        [1, 0, 1],
        [1, 0, -1],
        [-1, 0, 1],
        [-1, 0, -1],
        [0, 1, 1],
        [0, 1, -1],
        [0, -1, 1],
        [0, -1, -1],
    ]
)
LATTICE_WEIGHTS = np.array([1.0 / 3.0] + [1.0 / 18.0] * 6 + [1.0 / 36.0] * 12)
OPPOSITE = np.array([0, 2, 1, 4, 3, 6, 5, 10, 9, 8, 7, 14, 13, 12, 11, 18, 17, 16, 15])
OMEGA_BASE = 1.0
OMEGA_SPAN = 0.8
SENS_SCALE = 10.0

W32 = [float(np.float32(w)) for w in LATTICE_WEIGHTS]
XP = [i for i in range(19) if VELOCITIES[i, 0] == 1]
XM = [i for i in range(19) if VELOCITIES[i, 0] == -1]
YP = [i for i in range(19) if VELOCITIES[i, 1] == 1]
YM = [i for i in range(19) if VELOCITIES[i, 1] == -1]
LANES = 128


def _build_pulled(adj_ref, rxp, rxm, ryp, rym, rc7, rc8, rc9, rc10, pl_ref):
    _, rows, flat = adj_ref.shape
    tiles = flat // LANES
    row = lax.broadcasted_iota(jnp.int32, (rows, flat), 0)
    rowh = lax.broadcasted_iota(jnp.int32, (rows, LANES), 0)
    lane = lax.broadcasted_iota(jnp.int32, (rows, LANES), 1)
    zl = lane % NZ
    corners = {7: rc7, 8: rc8, 9: rc9, 10: rc10}
    for i in range(19):
        cx, cy, cz = (int(c) for c in VELOCITIES[i])
        v = adj_ref[i]
        if cx == 1:
            j = XP.index(i)
            v = jnp.where(row == rows - 1, rxp[j : j + 1, :], pltpu.roll(v, rows - 1, 0))
        elif cx == -1:
            j = XM.index(i)
            v = jnp.where(row == 0, rxm[j : j + 1, :], pltpu.roll(v, 1, 0))
        pieces = [v[:, LANES * t : LANES * (t + 1)] for t in range(tiles)]
        if cy != 0:
            h = ryp[YP.index(i)] if cy == 1 else rym[YM.index(i)]
            if cx == 1:
                h = jnp.where(rowh == rows - 1, corners[i][...], pltpu.roll(h, rows - 1, 0))
            elif cx == -1:
                h = jnp.where(rowh == 0, corners[i][...], pltpu.roll(h, 1, 0))
            if cy == 1:
                r = [pltpu.roll(p, LANES - NZ, 1) for p in pieces] + [pltpu.roll(h, LANES - NZ, 1)]
                pieces = [jnp.where(lane >= LANES - NZ, r[t + 1], r[t]) for t in range(tiles)]
            else:
                r = [pltpu.roll(h, NZ, 1)] + [pltpu.roll(p, NZ, 1) for p in pieces]
                pieces = [jnp.where(lane < NZ, r[t], r[t + 1]) for t in range(tiles)]
        if cz == 1:
            pieces = [
                jnp.where(zl == NZ - 1, pltpu.roll(p, NZ - 1, 1), pltpu.roll(p, LANES - 1, 1))
                for p in pieces
            ]
        elif cz == -1:
            pieces = [
                jnp.where(zl == 0, pltpu.roll(p, LANES - NZ + 1, 1), pltpu.roll(p, 1, 1))
                for p in pieces
            ]
        for t in range(tiles):
            pl_ref[i, :, LANES * t : LANES * (t + 1)] = pieces[t]


def _collide_vjp(f, g, rate, solid):
    rho = f[0]
    for i in range(1, 19):
        rho = rho + f[i]
    mom = []
    for a in range(3):
        pos = [f[i] for i in range(19) if VELOCITIES[i, a] > 0]
        neg = [f[i] for i in range(19) if VELOCITIES[i, a] < 0]
        acc = pos[0]
        for x in pos[1:]:
            acc = acc + x
        for x in neg:
            acc = acc - x
        mom.append(acc)
    u = [m / rho for m in mom]
    usq = u[0] * u[0] + u[1] * u[1] + u[2] * u[2]
    base = 1.0 - 1.5 * usq
    fluid = solid == 0
    one_minus = 1.0 - rate
    rbar = None
    esum = None
    easum = None
    mb = [None, None, None]
    proj = []
    amp = []
    gf = []
    for i in range(19):
        cvec = [int(c) for c in VELOCITIES[i]]
        p = None
        for a in range(3):
            if cvec[a] == 0:
                continue
            term = u[a] if cvec[a] > 0 else -u[a]
            p = term if p is None else p + term
        if p is None:
            amp_i = base
        else:
            amp_i = base + (3.0 + 4.5 * p) * p
        proj.append(p)
        amp.append(amp_i)
        gi = jnp.where(fluid, g[i], 0.0)
        gf.append(gi)
        feq = W32[i] * rho * amp_i
        t = gi * (feq - f[i])
        rbar = t if rbar is None else rbar + t
        e = (rate * W32[i]) * gi
        esum = e if esum is None else esum + e
        ea = e * amp_i
        easum = ea if easum is None else easum + ea
        if p is not None:
            ep = e * (3.0 + 9.0 * p)
            for a in range(3):
                if cvec[a] == 0:
                    continue
                if mb[a] is None:
                    mb[a] = ep if cvec[a] > 0 else -ep
                else:
                    mb[a] = mb[a] + ep if cvec[a] > 0 else mb[a] - ep
    mb = [mb[a] - 3.0 * u[a] * esum for a in range(3)]
    rhobar = easum - (mb[0] * u[0] + mb[1] * u[1] + mb[2] * u[2])
    out = []
    for i in range(19):
        cvec = [int(c) for c in VELOCITIES[i]]
        val = one_minus * gf[i] + rhobar
        for a in range(3):
            if cvec[a] > 0:
                val = val + mb[a]
            elif cvec[a] < 0:
                val = val - mb[a]
        out.append(jnp.where(fluid, val, g[int(OPPOSITE[i])]))
    return out, rbar


def _write_sends(out_ref, sxm, sxp, sym, syp, s7, s8, s9, s10):
    _, rows, flat = out_ref.shape
    sxm[...] = jnp.zeros(sxm.shape, jnp.float32)
    sxp[...] = jnp.zeros(sxp.shape, jnp.float32)
    for j, i in enumerate(XP):
        sxm[j : j + 1, :] = out_ref[i, 0:1, :]
    for j, i in enumerate(XM):
        sxp[j : j + 1, :] = out_ref[i, rows - 1 : rows, :]
    for j, i in enumerate(YP):
        sym[j] = out_ref[i, :, 0:LANES]
    for j, i in enumerate(YM):
        syp[j] = out_ref[i, :, flat - LANES : flat]
    s7[...] = out_ref[7, 0:1, 0:LANES]
    s8[...] = out_ref[8, 0:1, flat - LANES : flat]
    s9[...] = out_ref[9, rows - 1 : rows, 0:LANES]
    s10[...] = out_ref[10, rows - 1 : rows, flat - LANES : flat]


def _step_kernel(first, last, *refs):
    pops_ref, adj_ref, solid_ref, mask_ref, field_ref = refs[:5]
    halo = refs[5:13]
    k = 13
    if first:
        sens_in = None
    else:
        sens_in = refs[k]
        k += 1
    out_ref, sens_out = refs[k], refs[k + 1]
    sends = refs[k + 2 : k + 10] if not last else None
    pl_ref = refs[-1]
    _build_pulled(adj_ref, *halo, pl_ref)
    _, rows, flat = adj_ref.shape
    for t in range(flat // LANES):
        sl = slice(LANES * t, LANES * (t + 1))
        f = [pops_ref[0, i, :, sl].astype(jnp.float32) * W32[i] for i in range(19)]
        g = [pl_ref[i, :, sl] for i in range(19)]
        mask = mask_ref[:, sl].astype(jnp.float32)
        rate = OMEGA_BASE + OMEGA_SPAN * field_ref[:, sl] * mask
        solid = solid_ref[:, sl]
        new, rbar = _collide_vjp(f, g, rate, solid)
        for i in range(19):
            out_ref[i, :, sl] = new[i]
        contrib = SENS_SCALE * OMEGA_SPAN * mask * jnp.where(solid == 0, rbar, 0.0)
        if first:
            sens_out[:, sl] = contrib
        else:
            sens_out[:, sl] = sens_in[:, sl] + contrib
    if not last:
        _write_sends(out_ref, *sends)


def _pack_kernel(adj_ref, *sends):
    _write_sends(adj_ref, *sends)


def _full(shape):
    nd = len(shape)
    return pl.BlockSpec(shape, lambda i, _n=nd: (0,) * _n)


def _send_shapes(rows, flat):
    return [
        (8, flat),
        (8, flat),
        (len(YP), rows, LANES),
        (len(YM), rows, LANES),
        (1, LANES),
        (1, LANES),
        (1, LANES),
        (1, LANES),
    ]


def _pack(adj):
    _, rows, flat = adj.shape
    shapes = _send_shapes(rows, flat)
    return pl.pallas_call(
        _pack_kernel,
        grid=(1,),
        in_specs=[_full(adj.shape)],
        out_specs=[_full(s) for s in shapes],
        out_shape=[jax.ShapeDtypeStruct(s, jnp.float32) for s in shapes],
    )(adj)


def _step(step, first, last, saved_pops, adj, solid, mask, field, halo, sens):
    _, rows, flat = adj.shape
    shapes = _send_shapes(rows, flat)
    args = [saved_pops, adj, solid, mask, field] + list(halo)
    in_specs = [pl.BlockSpec((1, 19, rows, flat), lambda i, _s=step: (_s, 0, 0, 0))]
    in_specs += [_full(a.shape) for a in args[1:]]
    aliases = {}
    if not first:
        aliases = {len(args): 1}
        args.append(sens)
        in_specs.append(_full(sens.shape))
    out_shapes = [adj.shape, (rows, flat)] + ([] if last else shapes)
    kernel = lambda *refs: _step_kernel(first, last, *refs)
    return pl.pallas_call(
        kernel,
        grid=(1,),
        in_specs=in_specs,
        out_specs=[_full(s) for s in out_shapes],
        out_shape=[jax.ShapeDtypeStruct(s, jnp.float32) for s in out_shapes],
        scratch_shapes=[pltpu.VMEM(adj.shape, jnp.float32)],
        input_output_aliases=aliases,
    )(*args)


def _exchange(sends):
    nx = lax.axis_size("gx")
    ny = lax.axis_size("gy")
    sxm, sxp, sym, syp, s7, s8, s9, s10 = sends

    def shift(n, d):
        return [(i, (i + d) % n) for i in range(n)]

    def diag(dx, dy):
        return [
            (i * ny + j, ((i + dx) % nx) * ny + (j + dy) % ny) for i in range(nx) for j in range(ny)
        ]

    rxp = lax.ppermute(sxm, "gx", shift(nx, -1))
    rxm = lax.ppermute(sxp, "gx", shift(nx, 1))
    ryp = lax.ppermute(sym, "gy", shift(ny, -1))
    rym = lax.ppermute(syp, "gy", shift(ny, 1))
    both = ("gx", "gy")
    rc7 = lax.ppermute(s7, both, diag(-1, -1))
    rc8 = lax.ppermute(s8, both, diag(-1, 1))
    rc9 = lax.ppermute(s9, both, diag(1, -1))
    rc10 = lax.ppermute(s10, both, diag(1, 1))
    return [rxp, rxm, ryp, rym, rc7, rc8, rc9, rc10]


def body(saved_pops, seed_adjoint, solid_label, design_mask, design_field):
    num_steps = saved_pops.shape[0]
    adjoint = seed_adjoint
    sensitivity = None
    halo = _exchange(_pack(adjoint))
    for n, step in enumerate(reversed(range(num_steps))):
        first = n == 0
        last = step == 0
        outs = _step(
            step, first, last, saved_pops, adjoint, solid_label, design_mask, design_field, halo,
            sensitivity,
        )
        adjoint, sensitivity = outs[0], outs[1]
        if not last:
            halo = _exchange(outs[2:])
    return (adjoint, sensitivity)


def solution(mesh):
    in_specs = (
        P(None, None, "gx", "gy"),
        P(None, "gx", "gy"),
        P("gx", "gy"),
        P("gx", "gy"),
        P("gx", "gy"),
    )
    out_specs = (P(None, "gx", "gy"), P("gx", "gy"))
    return jax.shard_map(body, mesh=mesh, in_specs=in_specs, out_specs=out_specs, check_vma=False)
```

profile of v0, /device:TPU:0, one launch (start us, length us, event | category | flops | bytes accessed | tf_op | source)
XLA Modules:
  0.0 147.8 jit_solution(8464846418949412024)
XLA Ops:
  0.6 1.7 %shard_map.68 = (f32[8,512]{1,0:T(8,128)}, f32[8,512]{1,0:T(8,128)}, f32[5,16,128]{2,1,0:T(8,128)}, f32[5,16,128]{2,1,0:T(8,128)}, f32[1,128]{1,0:T(1,128)}, /*i...) custom-call(f32[19,16,512]{2,1,0:T(8,128)} %refs_1_.1), custom_call_target="tpu_custom_call" | custom-call | tf_op jit(solution)/shard_map/pallas_call | solution.py:242
  2.4 2.9 %collective-permute-start.2 = (f32[5,16,128]{2,1,0:T(8,128)}, f32[5,16,128]{2,1,0:T(8,128)S(1)}, u32[]{:S(2)}, u32[]{:S(2)}) collective-permute-start(f32[5,16,128]{2,1,0:T(8,128)} %get-tuple-element.42), channel_id=1, source_target_pairs={{0,31},{1,0},{2,1},{3,2},{4,3},{5,4},{6,5},{7,6},{8,7},{9,8},{10,9... | collective-permute-start | bytes 122888 | tf_op jit(solution)/shard_map/ppermute | solution.py:290
  5.3 5.9 %collective-permute-start = (f32[8,512]{1,0:T(8,128)}, f32[8,512]{1,0:T(8,128)S(1)}, u32[]{:S(2)}, u32[]{:S(2)}) collective-permute-start(f32[8,512]{1,0:T(8,128)} %get-tuple-element.40), channel_id=1, source_target_pairs={{0,224},{32,0},{64,32},{96,64},{128,96},{160,128},{192,160},{224,1... | collective-permute-start | bytes 49160 | tf_op jit(solution)/shard_map/ppermute | solution.py:288
  11.1 7.2 %collective-permute-start.4 = (f32[1,128]{1,0:T(1,128)}, f32[1,128]{1,0:T(1,128)S(1)}, u32[]{:S(2)}, u32[]{:S(2)}) collective-permute-start(f32[1,128]{1,0:T(1,128)} %get-tuple-element.44), channel_id=1, source_target_pairs={{0,255},{1,224},{2,225},{3,226},{4,227},{5,228},{6,229},{7,230},{8... | collective-permute-start | bytes 1544 | tf_op jit(solution)/shard_map/ppermute | solution.py:293
  19.8 7.4 %collective-permute-done.5.refs_10_ = f32[1,128]{1,0:T(1,128)S(1)} collective-permute-done((f32[1,128]{1,0:T(1,128)}, f32[1,128]{1,0:T(1,128)S(1)}, u32[]{:S(2)}, u32[]{:S(2)}) %collective-permute-start.5) | collective-permute-done | bytes 544 | tf_op jit(solution)/shard_map/ppermute | solution.py:294
  27.2 4.2 %collective-permute-done.6.refs_11_ = f32[1,128]{1,0:T(1,128)S(1)} collective-permute-done((f32[1,128]{1,0:T(1,128)}, f32[1,128]{1,0:T(1,128)S(1)}, u32[]{:S(2)}, u32[]{:S(2)}) %collective-permute-start.6) | collective-permute-done | bytes 544 | tf_op jit(solution)/shard_map/ppermute | solution.py:295
  31.5 8.6 %collective-permute-done.7.refs_12_ = f32[1,128]{1,0:T(1,128)S(1)} collective-permute-done((f32[1,128]{1,0:T(1,128)}, f32[1,128]{1,0:T(1,128)S(1)}, u32[]{:S(2)}, u32[]{:S(2)}) %collective-permute-start.7) | collective-permute-done | bytes 544 | tf_op jit(solution)/shard_map/ppermute | solution.py:296
  41.3 2.9 %shard_map.69 = (f32[19,16,512]{2,1,0:T(8,128)}, f32[16,512]{1,0:T(8,128)}, f32[8,512]{1,0:T(8,128)}, f32[8,512]{1,0:T(8,128)}, f32[5,16,128]{2,1,0:T(8,128)}, /...) custom-call(bf16[4,19,16,512]{3,2,1,0:T(8,128)(2,1)} %refs_0_.7, ...), custom_call_target="tpu_custom_call" | custom-call | tf_op jit(solution)/shard_map/pallas_call | solution.py:264
  46.8 6.7 %collective-permute-start.12 = (f32[1,128]{1,0:T(1,128)}, f32[1,128]{1,0:T(1,128)S(1)}, u32[]{:S(2)}, u32[]{:S(2)}) collective-permute-start(f32[1,128]{1,0:T(1,128)} %get-tuple-element.53), channel_id=1, source_target_pairs={{0,255},{1,224},{2,225},{3,226},{4,227},{5,228},{6,229},{7,230},{8... | collective-permute-start | bytes 1544 | tf_op jit(solution)/shard_map/ppermute | solution.py:293
  54.9 7.2 %collective-permute-done.13.refs_10_ = f32[1,128]{1,0:T(1,128)S(1)} collective-permute-done((f32[1,128]{1,0:T(1,128)}, f32[1,128]{1,0:T(1,128)S(1)}, u32[]{:S(2)}, u32[]{:S(2)}) %collective-permute-start.13) | collective-permute-done | bytes 544 | tf_op jit(solution)/shard_map/ppermute | solution.py:294
  62.1 4.4 %collective-permute-done.14.refs_11_ = f32[1,128]{1,0:T(1,128)S(1)} collective-permute-done((f32[1,128]{1,0:T(1,128)}, f32[1,128]{1,0:T(1,128)S(1)}, u32[]{:S(2)}, u32[]{:S(2)}) %collective-permute-start.14) | collective-permute-done | bytes 544 | tf_op jit(solution)/shard_map/ppermute | solution.py:295
  66.5 8.6 %collective-permute-done.15.refs_12_ = f32[1,128]{1,0:T(1,128)S(1)} collective-permute-done((f32[1,128]{1,0:T(1,128)}, f32[1,128]{1,0:T(1,128)S(1)}, u32[]{:S(2)}, u32[]{:S(2)}) %collective-permute-start.15) | collective-permute-done | bytes 544 | tf_op jit(solution)/shard_map/ppermute | solution.py:296
  75.8 2.9 %shard_map.70 = (f32[19,16,512]{2,1,0:T(8,128)}, f32[16,512]{1,0:T(8,128)}, f32[8,512]{1,0:T(8,128)}, f32[8,512]{1,0:T(8,128)}, f32[5,16,128]{2,1,0:T(8,128)}, /...) custom-call(bf16[4,19,16,512]{3,2,1,0:T(8,128)(2,1)} %refs_0_.7, ...), custom_call_target="tpu_custom_call", output_to_operand_aliasing={{1}: (13, {})} | custom-call | tf_op jit(solution)/shard_map/pallas_call | solution.py:264
  81.3 6.7 %collective-permute-start.20 = (f32[1,128]{1,0:T(1,128)}, f32[1,128]{1,0:T(1,128)S(1)}, u32[]{:S(2)}, u32[]{:S(2)}) collective-permute-start(f32[1,128]{1,0:T(1,128)} %get-tuple-element.63), channel_id=1, source_target_pairs={{0,255},{1,224},{2,225},{3,226},{4,227},{5,228},{6,229},{7,230},{8... | collective-permute-start | bytes 1544 | tf_op jit(solution)/shard_map/ppermute | solution.py:293
  89.4 7.2 %collective-permute-done.21.refs_10_ = f32[1,128]{1,0:T(1,128)S(1)} collective-permute-done((f32[1,128]{1,0:T(1,128)}, f32[1,128]{1,0:T(1,128)S(1)}, u32[]{:S(2)}, u32[]{:S(2)}) %collective-permute-start.21) | collective-permute-done | bytes 544 | tf_op jit(solution)/shard_map/ppermute | solution.py:294
  96.6 4.2 %collective-permute-done.22.refs_11_ = f32[1,128]{1,0:T(1,128)S(1)} collective-permute-done((f32[1,128]{1,0:T(1,128)}, f32[1,128]{1,0:T(1,128)S(1)}, u32[]{:S(2)}, u32[]{:S(2)}) %collective-permute-start.22) | collective-permute-done | bytes 544 | tf_op jit(solution)/shard_map/ppermute | solution.py:295
  100.9 8.8 %collective-permute-done.23.refs_12_ = f32[1,128]{1,0:T(1,128)S(1)} collective-permute-done((f32[1,128]{1,0:T(1,128)}, f32[1,128]{1,0:T(1,128)S(1)}, u32[]{:S(2)}, u32[]{:S(2)}) %collective-permute-start.23) | collective-permute-done | bytes 544 | tf_op jit(solution)/shard_map/ppermute | solution.py:296
  110.4 2.9 %shard_map.71 = (f32[19,16,512]{2,1,0:T(8,128)}, f32[16,512]{1,0:T(8,128)}, f32[8,512]{1,0:T(8,128)}, f32[8,512]{1,0:T(8,128)}, f32[5,16,128]{2,1,0:T(8,128)}, /...) custom-call(bf16[4,19,16,512]{3,2,1,0:T(8,128)(2,1)} %refs_0_.7, ...), custom_call_target="tpu_custom_call", output_to_operand_aliasing={{1}: (13, {})} | custom-call | tf_op jit(solution)/shard_map/pallas_call | solution.py:264
  113.9 1.6 %collective-permute-start.24 = (f32[8,512]{1,0:T(8,128)}, f32[8,512]{1,0:T(8,128)S(1)}, u32[]{:S(2)}, u32[]{:S(2)}) collective-permute-start(f32[8,512]{1,0:T(8,128)} %get-tuple-element.69), channel_id=1, source_target_pairs={{0,224},{32,0},{64,32},{96,64},{128,96},{160,128},{192,160},{224,1... | collective-permute-start | bytes 49160 | tf_op jit(solution)/shard_map/ppermute | solution.py:288
  115.9 6.8 %collective-permute-start.28 = (f32[1,128]{1,0:T(1,128)}, f32[1,128]{1,0:T(1,128)S(1)}, u32[]{:S(2)}, u32[]{:S(2)}) collective-permute-start(f32[1,128]{1,0:T(1,128)} %get-tuple-element.73), channel_id=1, source_target_pairs={{0,255},{1,224},{2,225},{3,226},{4,227},{5,228},{6,229},{7,230},{8... | collective-permute-start | bytes 1544 | tf_op jit(solution)/shard_map/ppermute | solution.py:293
  124.0 7.4 %collective-permute-done.29.refs_10_ = f32[1,128]{1,0:T(1,128)S(1)} collective-permute-done((f32[1,128]{1,0:T(1,128)}, f32[1,128]{1,0:T(1,128)S(1)}, u32[]{:S(2)}, u32[]{:S(2)}) %collective-permute-start.29) | collective-permute-done | bytes 544 | tf_op jit(solution)/shard_map/ppermute | solution.py:294
  131.4 4.2 %collective-permute-done.30.refs_11_ = f32[1,128]{1,0:T(1,128)S(1)} collective-permute-done((f32[1,128]{1,0:T(1,128)}, f32[1,128]{1,0:T(1,128)S(1)}, u32[]{:S(2)}, u32[]{:S(2)}) %collective-permute-start.30) | collective-permute-done | bytes 544 | tf_op jit(solution)/shard_map/ppermute | solution.py:295
  135.7 8.6 %collective-permute-done.31.refs_12_ = f32[1,128]{1,0:T(1,128)S(1)} collective-permute-done((f32[1,128]{1,0:T(1,128)}, f32[1,128]{1,0:T(1,128)S(1)}, u32[]{:S(2)}, u32[]{:S(2)}) %collective-permute-start.31) | collective-permute-done | bytes 544 | tf_op jit(solution)/shard_map/ppermute | solution.py:296
  145.0 2.8 %shard_map.72 = (f32[19,16,512]{2,1,0:T(8,128)}, f32[16,512]{1,0:T(8,128)}) custom-call(bf16[4,19,16,512]{3,2,1,0:T(8,128)(2,1)} %refs_0_.7, f32[19,16,512]{2,1,0:T(8,128)} %get-tuple-element.68.refs_1_, s32[16,512]{1,0:T(8,128)} %refs_2_.7, s32[16,512]{1,0:T(8,128)} %refs_3_.7, f32[16,512]{1,0:T(8,128)} %refs_4_.7, ...), custom_call_target="tpu_custom_call", output_to_operand_aliasing={{1}: (13, {})} | custom-call | tf_op jit(solution)/shard_map/pallas_call | solution.py:264
  (109 shorter events, 14.8 us)
Async XLA Ops:
  2.4 37.7 %collective-permute-start.2 = (f32[5,16,128]{2,1,0:T(8,128)}, f32[5,16,128]{2,1,0:T(8,128)S(1)}, u32[]{:S(2)}, u32[]{:S(2)}) collective-permute-start(f32[5,16,128]{2,1,0:T(8,128)} %get-tuple-element.42), channel_id=1, source_target_pairs={{0,31},{1,0},{2,1},{3,2},{4,3},{5,4},{6,5},{7,6},{8,7},{9,8},{10,9... | collective-permute-start | bytes 122888 | tf_op jit(solution)/shard_map/ppermute | solution.py:290
  5.3 34.8 %collective-permute-start.3 = (f32[5,16,128]{2,1,0:T(8,128)}, f32[5,16,128]{2,1,0:T(8,128)S(1)}, u32[]{:S(2)}, u32[]{:S(2)}) collective-permute-start(f32[5,16,128]{2,1,0:T(8,128)} %get-tuple-element.43), channel_id=1, source_target_pairs={{0,1},{1,2},{2,3},{3,4},{4,5},{5,6},{6,7},{7,8},{8,9},{9,10},{10,1... | collective-permute-start | bytes 122888 | tf_op jit(solution)/shard_map/ppermute | solution.py:291
  5.3 34.8 %collective-permute-start = (f32[8,512]{1,0:T(8,128)}, f32[8,512]{1,0:T(8,128)S(1)}, u32[]{:S(2)}, u32[]{:S(2)}) collective-permute-start(f32[8,512]{1,0:T(8,128)} %get-tuple-element.40), channel_id=1, source_target_pairs={{0,224},{32,0},{64,32},{96,64},{128,96},{160,128},{192,160},{224,1... | collective-permute-start | bytes 49160 | tf_op jit(solution)/shard_map/ppermute | solution.py:288
  11.1 28.9 %collective-permute-start.1 = (f32[8,512]{1,0:T(8,128)}, f32[8,512]{1,0:T(8,128)S(1)}, u32[]{:S(2)}, u32[]{:S(2)}) collective-permute-start(f32[8,512]{1,0:T(8,128)} %get-tuple-element.41), channel_id=1, source_target_pairs={{0,32},{32,64},{64,96},{96,128},{128,160},{160,192},{192,224},{224... | collective-permute-start | bytes 49160 | tf_op jit(solution)/shard_map/ppermute | solution.py:289
  11.1 8.7 %collective-permute-start.4 = (f32[1,128]{1,0:T(1,128)}, f32[1,128]{1,0:T(1,128)S(1)}, u32[]{:S(2)}, u32[]{:S(2)}) collective-permute-start(f32[1,128]{1,0:T(1,128)} %get-tuple-element.44), channel_id=1, source_target_pairs={{0,255},{1,224},{2,225},{3,226},{4,227},{5,228},{6,229},{7,230},{8... | collective-permute-start | bytes 1544 | tf_op jit(solution)/shard_map/ppermute | solution.py:293
  31.5 8.6 %collective-permute-start.7 = (f32[1,128]{1,0:T(1,128)}, f32[1,128]{1,0:T(1,128)S(1)}, u32[]{:S(2)}, u32[]{:S(2)}) collective-permute-start(f32[1,128]{1,0:T(1,128)} %get-tuple-element.47), channel_id=1, source_target_pairs={{0,33},{1,34},{2,35},{3,36},{4,37},{5,38},{6,39},{7,40},{8,41},{9,... | collective-permute-start | bytes 1544 | tf_op jit(solution)/shard_map/ppermute | solution.py:296
  44.2 31.0 %collective-permute-start.10 = (f32[5,16,128]{2,1,0:T(8,128)}, f32[5,16,128]{2,1,0:T(8,128)S(1)}, u32[]{:S(2)}, u32[]{:S(2)}) collective-permute-start(f32[5,16,128]{2,1,0:T(8,128)} %get-tuple-element.51), channel_id=1, source_target_pairs={{0,31},{1,0},{2,1},{3,2},{4,3},{5,4},{6,5},{7,6},{8,7},{9,8},{10,9... | collective-permute-start | bytes 122888 | tf_op jit(solution)/shard_map/ppermute | solution.py:290
  44.3 30.9 %collective-permute-start.11 = (f32[5,16,128]{2,1,0:T(8,128)}, f32[5,16,128]{2,1,0:T(8,128)S(1)}, u32[]{:S(2)}, u32[]{:S(2)}) collective-permute-start(f32[5,16,128]{2,1,0:T(8,128)} %get-tuple-element.52), channel_id=1, source_target_pairs={{0,1},{1,2},{2,3},{3,4},{4,5},{5,6},{6,7},{7,8},{8,9},{9,10},{10,1... | collective-permute-start | bytes 122888 | tf_op jit(solution)/shard_map/ppermute | solution.py:291
  44.8 30.4 %collective-permute-start.8 = (f32[8,512]{1,0:T(8,128)}, f32[8,512]{1,0:T(8,128)S(1)}, u32[]{:S(2)}, u32[]{:S(2)}) collective-permute-start(f32[8,512]{1,0:T(8,128)} %get-tuple-element.49), channel_id=1, source_target_pairs={{0,224},{32,0},{64,32},{96,64},{128,96},{160,128},{192,160},{224,1... | collective-permute-start | bytes 49160 | tf_op jit(solution)/shard_map/ppermute | solution.py:288
  46.4 28.8 %collective-permute-start.9 = (f32[8,512]{1,0:T(8,128)}, f32[8,512]{1,0:T(8,128)S(1)}, u32[]{:S(2)}, u32[]{:S(2)}) collective-permute-start(f32[8,512]{1,0:T(8,128)} %get-tuple-element.50), channel_id=1, source_target_pairs={{0,32},{32,64},{64,96},{96,128},{128,160},{160,192},{192,224},{224... | collective-permute-start | bytes 49160 | tf_op jit(solution)/shard_map/ppermute | solution.py:289
  46.8 8.1 %collective-permute-start.12 = (f32[1,128]{1,0:T(1,128)}, f32[1,128]{1,0:T(1,128)S(1)}, u32[]{:S(2)}, u32[]{:S(2)}) collective-permute-start(f32[1,128]{1,0:T(1,128)} %get-tuple-element.53), channel_id=1, source_target_pairs={{0,255},{1,224},{2,225},{3,226},{4,227},{5,228},{6,229},{7,230},{8... | collective-permute-start | bytes 1544 | tf_op jit(solution)/shard_map/ppermute | solution.py:293
  66.5 8.6 %collective-permute-start.15 = (f32[1,128]{1,0:T(1,128)}, f32[1,128]{1,0:T(1,128)S(1)}, u32[]{:S(2)}, u32[]{:S(2)}) collective-permute-start(f32[1,128]{1,0:T(1,128)} %get-tuple-element.56), channel_id=1, source_target_pairs={{0,33},{1,34},{2,35},{3,36},{4,37},{5,38},{6,39},{7,40},{8,41},{9,... | collective-permute-start | bytes 1544 | tf_op jit(solution)/shard_map/ppermute | solution.py:296
  78.7 31.0 %collective-permute-start.18 = (f32[5,16,128]{2,1,0:T(8,128)}, f32[5,16,128]{2,1,0:T(8,128)S(1)}, u32[]{:S(2)}, u32[]{:S(2)}) collective-permute-start(f32[5,16,128]{2,1,0:T(8,128)} %get-tuple-element.61), channel_id=1, source_target_pairs={{0,31},{1,0},{2,1},{3,2},{4,3},{5,4},{6,5},{7,6},{8,7},{9,8},{10,9... | collective-permute-start | bytes 122888 | tf_op jit(solution)/shard_map/ppermute | solution.py:290
  78.8 31.0 %collective-permute-start.19 = (f32[5,16,128]{2,1,0:T(8,128)}, f32[5,16,128]{2,1,0:T(8,128)S(1)}, u32[]{:S(2)}, u32[]{:S(2)}) collective-permute-start(f32[5,16,128]{2,1,0:T(8,128)} %get-tuple-element.62), channel_id=1, source_target_pairs={{0,1},{1,2},{2,3},{3,4},{4,5},{5,6},{6,7},{7,8},{8,9},{9,10},{10,1... | collective-permute-start | bytes 122888 | tf_op jit(solution)/shard_map/ppermute | solution.py:291
  79.3 30.4 %collective-permute-start.16 = (f32[8,512]{1,0:T(8,128)}, f32[8,512]{1,0:T(8,128)S(1)}, u32[]{:S(2)}, u32[]{:S(2)}) collective-permute-start(f32[8,512]{1,0:T(8,128)} %get-tuple-element.59), channel_id=1, source_target_pairs={{0,224},{32,0},{64,32},{96,64},{128,96},{160,128},{192,160},{224,1... | collective-permute-start | bytes 49160 | tf_op jit(solution)/shard_map/ppermute | solution.py:288
  80.9 28.9 %collective-permute-start.17 = (f32[8,512]{1,0:T(8,128)}, f32[8,512]{1,0:T(8,128)S(1)}, u32[]{:S(2)}, u32[]{:S(2)}) collective-permute-start(f32[8,512]{1,0:T(8,128)} %get-tuple-element.60), channel_id=1, source_target_pairs={{0,32},{32,64},{64,96},{96,128},{128,160},{160,192},{192,224},{224... | collective-permute-start | bytes 49160 | tf_op jit(solution)/shard_map/ppermute | solution.py:289
  81.3 8.1 %collective-permute-start.20 = (f32[1,128]{1,0:T(1,128)}, f32[1,128]{1,0:T(1,128)S(1)}, u32[]{:S(2)}, u32[]{:S(2)}) collective-permute-start(f32[1,128]{1,0:T(1,128)} %get-tuple-element.63), channel_id=1, source_target_pairs={{0,255},{1,224},{2,225},{3,226},{4,227},{5,228},{6,229},{7,230},{8... | collective-permute-start | bytes 1544 | tf_op jit(solution)/shard_map/ppermute | solution.py:293
  100.9 8.8 %collective-permute-start.23 = (f32[1,128]{1,0:T(1,128)}, f32[1,128]{1,0:T(1,128)S(1)}, u32[]{:S(2)}, u32[]{:S(2)}) collective-permute-start(f32[1,128]{1,0:T(1,128)} %get-tuple-element.66), channel_id=1, source_target_pairs={{0,33},{1,34},{2,35},{3,36},{4,37},{5,38},{6,39},{7,40},{8,41},{9,... | collective-permute-start | bytes 1544 | tf_op jit(solution)/shard_map/ppermute | solution.py:296
  113.3 31.0 %collective-permute-start.26 = (f32[5,16,128]{2,1,0:T(8,128)}, f32[5,16,128]{2,1,0:T(8,128)S(1)}, u32[]{:S(2)}, u32[]{:S(2)}) collective-permute-start(f32[5,16,128]{2,1,0:T(8,128)} %get-tuple-element.71), channel_id=1, source_target_pairs={{0,31},{1,0},{2,1},{3,2},{4,3},{5,4},{6,5},{7,6},{8,7},{9,8},{10,9... | collective-permute-start | bytes 122888 | tf_op jit(solution)/shard_map/ppermute | solution.py:290
  113.4 31.0 %collective-permute-start.27 = (f32[5,16,128]{2,1,0:T(8,128)}, f32[5,16,128]{2,1,0:T(8,128)S(1)}, u32[]{:S(2)}, u32[]{:S(2)}) collective-permute-start(f32[5,16,128]{2,1,0:T(8,128)} %get-tuple-element.72), channel_id=1, source_target_pairs={{0,1},{1,2},{2,3},{3,4},{4,5},{5,6},{6,7},{7,8},{8,9},{9,10},{10,1... | collective-permute-start | bytes 122888 | tf_op jit(solution)/shard_map/ppermute | solution.py:291
  113.9 30.4 %collective-permute-start.24 = (f32[8,512]{1,0:T(8,128)}, f32[8,512]{1,0:T(8,128)S(1)}, u32[]{:S(2)}, u32[]{:S(2)}) collective-permute-start(f32[8,512]{1,0:T(8,128)} %get-tuple-element.69), channel_id=1, source_target_pairs={{0,224},{32,0},{64,32},{96,64},{128,96},{160,128},{192,160},{224,1... | collective-permute-start | bytes 49160 | tf_op jit(solution)/shard_map/ppermute | solution.py:288
  115.5 28.8 %collective-permute-start.25 = (f32[8,512]{1,0:T(8,128)}, f32[8,512]{1,0:T(8,128)S(1)}, u32[]{:S(2)}, u32[]{:S(2)}) collective-permute-start(f32[8,512]{1,0:T(8,128)} %get-tuple-element.70), channel_id=1, source_target_pairs={{0,32},{32,64},{64,96},{96,128},{128,160},{160,192},{192,224},{224... | collective-permute-start | bytes 49160 | tf_op jit(solution)/shard_map/ppermute | solution.py:289
  115.9 8.1 %collective-permute-start.28 = (f32[1,128]{1,0:T(1,128)}, f32[1,128]{1,0:T(1,128)S(1)}, u32[]{:S(2)}, u32[]{:S(2)}) collective-permute-start(f32[1,128]{1,0:T(1,128)} %get-tuple-element.73), channel_id=1, source_target_pairs={{0,255},{1,224},{2,225},{3,226},{4,227},{5,228},{6,229},{7,230},{8... | collective-permute-start | bytes 1544 | tf_op jit(solution)/shard_map/ppermute | solution.py:293
  135.7 8.6 %collective-permute-start.31 = (f32[1,128]{1,0:T(1,128)}, f32[1,128]{1,0:T(1,128)S(1)}, u32[]{:S(2)}, u32[]{:S(2)}) collective-permute-start(f32[1,128]{1,0:T(1,128)} %get-tuple-element.76), channel_id=1, source_target_pairs={{0,33},{1,34},{2,35},{3,36},{4,37},{5,38},{6,39},{7,40},{8,41},{9,... | collective-permute-start | bytes 1544 | tf_op jit(solution)/shard_map/ppermute | solution.py:296
  (40 other events, 226.5 us)
where the time goes:
time: 148 us
  waiting for transfers between devices  86.6 us (59%)
  starting transfers between devices  44 us (30%)
  Pallas kernels  13.2 us (9%)
  local copies, waits for them, and re-layouts  2.98 us (2%)
    ppermute x4, waiting for transfers between devices, _exchange(): rc10 = lax.ppermute(s10, both, diag(1, 1))  34.6 us
    ppermute x4, waiting for transfers between devices, _exchange(): rc8 = lax.ppermute(s8, both, diag(-1, 1))  29.3 us
    ppermute x4, starting transfers between devices, _exchange(): rc7 = lax.ppermute(s7, both, diag(-1, -1))  27.4 us
    ppermute x4, waiting for transfers between devices, _exchange(): rc9 = lax.ppermute(s9, both, diag(1, -1))  17.1 us
    pallas_call x4, Pallas kernels, _step(): pl.pallas_call(kernel, grid=(1,), in_specs=in_specs, out_specs=[_full(s)...  11.5 us
    ppermute x4, starting transfers between devices, _exchange(): rxp = lax.ppermute(sxm, 'gx', shift(nx, -1))  10.6 us
    ppermute x4, waiting for transfers between devices, _exchange(): rc7 = lax.ppermute(s7, both, diag(-1, -1))  5.57 us
    ppermute x4, starting transfers between devices, _exchange(): ryp = lax.ppermute(sym, 'gy', shift(ny, -1))  3.16 us
  transfers between devices with their start and end apart: 32, of which 16 were waited for; matrix products, arithmetic and copies ran while one was open for 0% of the time, Pallas kernels for 0%

commit v1 on v0

--- a/solution.py
+++ b/solution.py
@@ -46,14 +46,20 @@
 LANES = 128
 
 
-def _build_pulled(adj_ref, rxp, rxm, ryp, rym, rc7, rc8, rc9, rc10, pl_ref):
+def _build_pulled(adj_ref, rxp, rxm, ryp, rym, f7, f8, f9, f10, pl_ref):
     _, rows, flat = adj_ref.shape
     tiles = flat // LANES
     row = lax.broadcasted_iota(jnp.int32, (rows, flat), 0)
     rowh = lax.broadcasted_iota(jnp.int32, (rows, LANES), 0)
     lane = lax.broadcasted_iota(jnp.int32, (rows, LANES), 1)
     zl = lane % NZ
-    corners = {7: rc7, 8: rc8, 9: rc9, 10: rc10}
+    flat_end = flat - LANES
+    corners = {
+        7: lambda: f7[XP.index(7) : XP.index(7) + 1, 0:LANES],
+        8: lambda: f8[XP.index(8) : XP.index(8) + 1, flat_end:flat],
+        9: lambda: f9[XM.index(9) : XM.index(9) + 1, 0:LANES],
+        10: lambda: f10[XM.index(10) : XM.index(10) + 1, flat_end:flat],
+    }
     for i in range(19):
         cx, cy, cz = (int(c) for c in VELOCITIES[i])
         v = adj_ref[i]
@@ -67,9 +73,9 @@
         if cy != 0:
             h = ryp[YP.index(i)] if cy == 1 else rym[YM.index(i)]
             if cx == 1:
-                h = jnp.where(rowh == rows - 1, corners[i][...], pltpu.roll(h, rows - 1, 0))
+                h = jnp.where(rowh == rows - 1, corners[i](), pltpu.roll(h, rows - 1, 0))
             elif cx == -1:
-                h = jnp.where(rowh == 0, corners[i][...], pltpu.roll(h, 1, 0))
+                h = jnp.where(rowh == 0, corners[i](), pltpu.roll(h, 1, 0))
             if cy == 1:
                 r = [pltpu.roll(p, LANES - NZ, 1) for p in pieces] + [pltpu.roll(h, LANES - NZ, 1)]
                 pieces = [jnp.where(lane >= LANES - NZ, r[t + 1], r[t]) for t in range(tiles)]
@@ -163,7 +169,7 @@
     return out, rbar
 
 
-def _write_sends(out_ref, sxm, sxp, sym, syp, s7, s8, s9, s10):
+def _write_sends(out_ref, sxm, sxp, sym, syp):
     _, rows, flat = out_ref.shape
     sxm[...] = jnp.zeros(sxm.shape, jnp.float32)
     sxp[...] = jnp.zeros(sxp.shape, jnp.float32)
@@ -175,10 +181,6 @@
         sym[j] = out_ref[i, :, 0:LANES]
     for j, i in enumerate(YM):
         syp[j] = out_ref[i, :, flat - LANES : flat]
-    s7[...] = out_ref[7, 0:1, 0:LANES]
-    s8[...] = out_ref[8, 0:1, flat - LANES : flat]
-    s9[...] = out_ref[9, rows - 1 : rows, 0:LANES]
-    s10[...] = out_ref[10, rows - 1 : rows, flat - LANES : flat]
 
 
 def _step_kernel(first, last, *refs):
@@ -191,7 +193,7 @@
         sens_in = refs[k]
         k += 1
     out_ref, sens_out = refs[k], refs[k + 1]
-    sends = refs[k + 2 : k + 10] if not last else None
+    sends = refs[k + 2 : k + 6] if not last else None
     pl_ref = refs[-1]
     _build_pulled(adj_ref, *halo, pl_ref)
     _, rows, flat = adj_ref.shape
@@ -224,16 +226,7 @@
 
 
 def _send_shapes(rows, flat):
-    return [
-        (8, flat),
-        (8, flat),
-        (len(YP), rows, LANES),
-        (len(YM), rows, LANES),
-        (1, LANES),
-        (1, LANES),
-        (1, LANES),
-        (1, LANES),
-    ]
+    return [(8, flat), (8, flat), (len(YP), rows, LANES), (len(YM), rows, LANES)]
 
 
 def _pack(adj):
@@ -275,26 +268,20 @@
 def _exchange(sends):
     nx = lax.axis_size("gx")
     ny = lax.axis_size("gy")
-    sxm, sxp, sym, syp, s7, s8, s9, s10 = sends
+    sxm, sxp, sym, syp = sends
 
     def shift(n, d):
         return [(i, (i + d) % n) for i in range(n)]
-
-    def diag(dx, dy):
-        return [
-            (i * ny + j, ((i + dx) % nx) * ny + (j + dy) % ny) for i in range(nx) for j in range(ny)
-        ]
 
     rxp = lax.ppermute(sxm, "gx", shift(nx, -1))
     rxm = lax.ppermute(sxp, "gx", shift(nx, 1))
     ryp = lax.ppermute(sym, "gy", shift(ny, -1))
     rym = lax.ppermute(syp, "gy", shift(ny, 1))
-    both = ("gx", "gy")
-    rc7 = lax.ppermute(s7, both, diag(-1, -1))
-    rc8 = lax.ppermute(s8, both, diag(-1, 1))
-    rc9 = lax.ppermute(s9, both, diag(1, -1))
-    rc10 = lax.ppermute(s10, both, diag(1, 1))
-    return [rxp, rxm, ryp, rym, rc7, rc8, rc9, rc10]
+    f7 = lax.ppermute(rxp, "gy", shift(ny, -1))
+    f8 = lax.ppermute(rxp, "gy", shift(ny, 1))
+    f9 = lax.ppermute(rxm, "gy", shift(ny, -1))
+    f10 = lax.ppermute(rxm, "gy", shift(ny, 1))
+    return [rxp, rxm, ryp, rym, f7, f8, f9, f10]
 
 
 def body(saved_pops, seed_adjoint, solid_label, design_mask, design_field):

time: 148 us -> 98.8 us (0.67)
  the two profiles are of different devices: /device:TPU:0 before, /device:TPU:31 now
where the time goes in v1:
time: 98.8 us; the launch traced here: 98.6 us
  starting transfers between devices  42.2 us (43%)
  waiting for transfers between devices  39.4 us (40%)
  Pallas kernels  13.2 us (13%)
  local copies, waits for them, and re-layouts  2.94 us (3%)
    ppermute x4, waiting for transfers between devices, _exchange(): f9 = lax.ppermute(rxm, 'gy', shift(ny, -1))  20.3 us
    ppermute x4, starting transfers between devices, _exchange(): rym = lax.ppermute(syp, 'gy', shift(ny, 1))  19.3 us
    ppermute x4, starting transfers between devices, _exchange(): rxp = lax.ppermute(sxm, 'gx', shift(nx, -1))  14.2 us
    ppermute x4, waiting for transfers between devices, _exchange(): rxm = lax.ppermute(sxp, 'gx', shift(nx, 1))  13.4 us
    pallas_call x4, Pallas kernels, _step(): pl.pallas_call(kernel, grid=(1,), in_specs=in_specs, out_specs=[_full(s)...  11.5 us
    ppermute x4, waiting for transfers between devices, _exchange(): f7 = lax.ppermute(rxp, 'gy', shift(ny, -1))  5.6 us
    ppermute x4, starting transfers between devices, _exchange(): f10 = lax.ppermute(rxm, 'gy', shift(ny, 1))  5.17 us
    unnamed x64, local copies, waits for them, and re-layouts  2.94 us
  transfers between devices with their start and end apart: 32, of which 12 were waited for; matrix products, arithmetic and copies ran while one was open for 0% of the time, Pallas kernels for 0%

profile of v1, /device:TPU:31, one launch (start us, length us, event | category | flops | bytes accessed | tf_op | source)
XLA Modules:
  0.0 98.6 jit_solution(379984120770911326)
XLA Ops:
  0.6 1.7 %shard_map.68 = (f32[8,512]{1,0:T(8,128)}, f32[8,512]{1,0:T(8,128)}, f32[5,16,128]{2,1,0:T(8,128)}, f32[5,16,128]{2,1,0:T(8,128)}) custom-call(f32[19,16,512]{2,1,0:T(8,128)} %refs_1_.1), custom_call_target="tpu_custom_call" | custom-call | tf_op jit(solution)/shard_map/pallas_call | solution.py:235
  2.3 5.6 %collective-permute-start = (f32[8,512]{1,0:T(8,128)}, f32[8,512]{1,0:T(8,128)S(1)}, u32[]{:S(2)}, u32[]{:S(2)}) collective-permute-start(f32[8,512]{1,0:T(8,128)} %get-tuple-element.24), channel_id=1, source_target_pairs={{0,224},{32,0},{64,32},{96,64},{128,96},{160,128},{192,160},{224,1... | collective-permute-start | bytes 49160 | tf_op jit(solution)/shard_map/ppermute | solution.py:276
  8.9 4.1 %collective-permute-start.3 = (f32[5,16,128]{2,1,0:T(8,128)}, f32[5,16,128]{2,1,0:T(8,128)S(1)}, u32[]{:S(2)}, u32[]{:S(2)}) collective-permute-start(f32[5,16,128]{2,1,0:T(8,128)} %get-tuple-element.27), channel_id=1, source_target_pairs={{0,1},{1,2},{2,3},{3,4},{4,5},{5,6},{6,7},{7,8},{8,9},{9,10},{10,1... | collective-permute-start | bytes 122888 | tf_op jit(solution)/shard_map/ppermute | solution.py:279
  13.6 3.4 %collective-permute-done.1.refs_6_ = f32[8,512]{1,0:T(8,128)S(1)} collective-permute-done((f32[8,512]{1,0:T(8,128)}, f32[8,512]{1,0:T(8,128)S(1)}, u32[]{:S(2)}, u32[]{:S(2)}) %collective-permute-start.1) | collective-permute-done | bytes 16416 | tf_op jit(solution)/shard_map/ppermute | solution.py:277
  18.3 1.4 %collective-permute-done.4.refs_9_ = f32[8,512]{1,0:T(8,128)S(1)} collective-permute-done((f32[8,512]{1,0:T(8,128)S(1)}, f32[8,512]{1,0:T(8,128)S(1)}, u32[]{:S(2)}, u32[]{:S(2)}) %collective-permute-start.4) | collective-permute-done | bytes 16416 | tf_op jit(solution)/shard_map/ppermute | solution.py:280
  19.7 5.1 %collective-permute-done.6.refs_11_ = f32[8,512]{1,0:T(8,128)S(1)} collective-permute-done((f32[8,512]{1,0:T(8,128)S(1)}, f32[8,512]{1,0:T(8,128)S(1)}, u32[]{:S(2)}, u32[]{:S(2)}) %collective-permute-start.6) | collective-permute-done | bytes 16416 | tf_op jit(solution)/shard_map/ppermute | solution.py:282
  26.0 2.9 %shard_map.69 = (f32[19,16,512]{2,1,0:T(8,128)}, f32[16,512]{1,0:T(8,128)}, f32[8,512]{1,0:T(8,128)}, f32[8,512]{1,0:T(8,128)}, f32[5,16,128]{2,1,0:T(8,128)}, /*index=5*/f32[5,16,128]{2,1,0:T(8,128)}) custom-call(bf16[4,19,16,512]{3,2,1,0:T(8,128)(2,1)} %refs_0_.7, f32[19,16,512]{2,1,0:T(8,128)} %refs_1_.1, s32[16,512]{1,0:T(8,128)} %refs_2_.7, ...), custom_call_target="tpu_custom_call" | custom-call | tf_op jit(solution)/shard_map/pallas_call | solution.py:257
  28.8 2.9 %collective-permute-start.8 = (f32[8,512]{1,0:T(8,128)}, f32[8,512]{1,0:T(8,128)S(1)}, u32[]{:S(2)}, u32[]{:S(2)}) collective-permute-start(f32[8,512]{1,0:T(8,128)} %get-tuple-element.29), channel_id=1, source_target_pairs={{0,224},{32,0},{64,32},{96,64},{128,96},{160,128},{192,160},{224,1... | collective-permute-start | bytes 49160 | tf_op jit(solution)/shard_map/ppermute | solution.py:276
  31.7 5.1 %collective-permute-start.11 = (f32[5,16,128]{2,1,0:T(8,128)}, f32[5,16,128]{2,1,0:T(8,128)S(1)}, u32[]{:S(2)}, u32[]{:S(2)}) collective-permute-start(f32[5,16,128]{2,1,0:T(8,128)} %get-tuple-element.32), channel_id=1, source_target_pairs={{0,1},{1,2},{2,3},{3,4},{4,5},{5,6},{6,7},{7,8},{8,9},{9,10},{10,1... | collective-permute-start | bytes 122888 | tf_op jit(solution)/shard_map/ppermute | solution.py:279
  37.4 3.4 %collective-permute-done.9.refs_6_ = f32[8,512]{1,0:T(8,128)S(1)} collective-permute-done((f32[8,512]{1,0:T(8,128)}, f32[8,512]{1,0:T(8,128)S(1)}, u32[]{:S(2)}, u32[]{:S(2)}) %collective-permute-start.9) | collective-permute-done | bytes 16416 | tf_op jit(solution)/shard_map/ppermute | solution.py:277
  43.4 5.1 %collective-permute-done.14.refs_11_ = f32[8,512]{1,0:T(8,128)S(1)} collective-permute-done((f32[8,512]{1,0:T(8,128)S(1)}, f32[8,512]{1,0:T(8,128)S(1)}, u32[]{:S(2)}, u32[]{:S(2)}) %collective-permute-start.14) | collective-permute-done | bytes 16416 | tf_op jit(solution)/shard_map/ppermute | solution.py:282
  49.1 2.9 %shard_map.70 = (f32[19,16,512]{2,1,0:T(8,128)}, f32[16,512]{1,0:T(8,128)}, f32[8,512]{1,0:T(8,128)}, f32[8,512]{1,0:T(8,128)}, f32[5,16,128]{2,1,0:T(8,128)}, /*index=5*/f32[5,16,128]{2,1,0:T(8,128)}) custom-call(bf16[4,19,16,512]{3,2,1,0:T(8,128)(2,1)} %refs_0_.7, f32[19,16,512]{2,1,0:T(8,128)} %get-tuple-element.28.refs_1_, ...), custom_call_target="tpu_custom_call", output_to_operand_aliasing={{1}: (13, {})} | custom-call | tf_op jit(solution)/shard_map/pallas_call | solution.py:257
  52.0 2.9 %collective-permute-start.16 = (f32[8,512]{1,0:T(8,128)}, f32[8,512]{1,0:T(8,128)S(1)}, u32[]{:S(2)}, u32[]{:S(2)}) collective-permute-start(f32[8,512]{1,0:T(8,128)} %get-tuple-element.35), channel_id=1, source_target_pairs={{0,224},{32,0},{64,32},{96,64},{128,96},{160,128},{192,160},{224,1... | collective-permute-start | bytes 49160 | tf_op jit(solution)/shard_map/ppermute | solution.py:276
  54.9 5.1 %collective-permute-start.19 = (f32[5,16,128]{2,1,0:T(8,128)}, f32[5,16,128]{2,1,0:T(8,128)S(1)}, u32[]{:S(2)}, u32[]{:S(2)}) collective-permute-start(f32[5,16,128]{2,1,0:T(8,128)} %get-tuple-element.38), channel_id=1, source_target_pairs={{0,1},{1,2},{2,3},{3,4},{4,5},{5,6},{6,7},{7,8},{8,9},{9,10},{10,1... | collective-permute-start | bytes 122888 | tf_op jit(solution)/shard_map/ppermute | solution.py:279
  60.6 3.4 %collective-permute-done.17.refs_6_ = f32[8,512]{1,0:T(8,128)S(1)} collective-permute-done((f32[8,512]{1,0:T(8,128)}, f32[8,512]{1,0:T(8,128)S(1)}, u32[]{:S(2)}, u32[]{:S(2)}) %collective-permute-start.17) | collective-permute-done | bytes 16416 | tf_op jit(solution)/shard_map/ppermute | solution.py:277
  65.2 1.4 %collective-permute-done.20.refs_9_ = f32[8,512]{1,0:T(8,128)S(1)} collective-permute-done((f32[8,512]{1,0:T(8,128)S(1)}, f32[8,512]{1,0:T(8,128)S(1)}, u32[]{:S(2)}, u32[]{:S(2)}) %collective-permute-start.20) | collective-permute-done | bytes 16416 | tf_op jit(solution)/shard_map/ppermute | solution.py:280
  66.6 5.1 %collective-permute-done.22.refs_11_ = f32[8,512]{1,0:T(8,128)S(1)} collective-permute-done((f32[8,512]{1,0:T(8,128)S(1)}, f32[8,512]{1,0:T(8,128)S(1)}, u32[]{:S(2)}, u32[]{:S(2)}) %collective-permute-start.22) | collective-permute-done | bytes 16416 | tf_op jit(solution)/shard_map/ppermute | solution.py:282
  72.4 2.9 %shard_map.71 = (f32[19,16,512]{2,1,0:T(8,128)}, f32[16,512]{1,0:T(8,128)}, f32[8,512]{1,0:T(8,128)}, f32[8,512]{1,0:T(8,128)}, f32[5,16,128]{2,1,0:T(8,128)}, /*index=5*/f32[5,16,128]{2,1,0:T(8,128)}) custom-call(bf16[4,19,16,512]{3,2,1,0:T(8,128)(2,1)} %refs_0_.7, f32[19,16,512]{2,1,0:T(8,128)} %get-tuple-element.34.refs_1_, ...), custom_call_target="tpu_custom_call", output_to_operand_aliasing={{1}: (13, {})} | custom-call | tf_op jit(solution)/shard_map/pallas_call | solution.py:257
  75.2 2.9 %collective-permute-start.24 = (f32[8,512]{1,0:T(8,128)}, f32[8,512]{1,0:T(8,128)S(1)}, u32[]{:S(2)}, u32[]{:S(2)}) collective-permute-start(f32[8,512]{1,0:T(8,128)} %get-tuple-element.41), channel_id=1, source_target_pairs={{0,224},{32,0},{64,32},{96,64},{128,96},{160,128},{192,160},{224,1... | collective-permute-start | bytes 49160 | tf_op jit(solution)/shard_map/ppermute | solution.py:276
  78.1 5.1 %collective-permute-start.27 = (f32[5,16,128]{2,1,0:T(8,128)}, f32[5,16,128]{2,1,0:T(8,128)S(1)}, u32[]{:S(2)}, u32[]{:S(2)}) collective-permute-start(f32[5,16,128]{2,1,0:T(8,128)} %get-tuple-element.44), channel_id=1, source_target_pairs={{0,1},{1,2},{2,3},{3,4},{4,5},{5,6},{6,7},{7,8},{8,9},{9,10},{10,1... | collective-permute-start | bytes 122888 | tf_op jit(solution)/shard_map/ppermute | solution.py:279
  84.0 3.2 %collective-permute-done.25.refs_6_ = f32[8,512]{1,0:T(8,128)S(1)} collective-permute-done((f32[8,512]{1,0:T(8,128)}, f32[8,512]{1,0:T(8,128)S(1)}, u32[]{:S(2)}, u32[]{:S(2)}) %collective-permute-start.25) | collective-permute-done | bytes 16416 | tf_op jit(solution)/shard_map/ppermute | solution.py:277
  87.2 1.5 %collective-permute-start.31 = (f32[8,512]{1,0:T(8,128)S(1)}, f32[8,512]{1,0:T(8,128)S(1)}, u32[]{:S(2)}, u32[]{:S(2)}) collective-permute-start(f32[8,512]{1,0:T(8,128)S(1)} %collective-permute-done.25.refs_6_), channel_id=1, source_target_pairs={{0,1},{1,2},{2,3},{3,4},{4,5},{5,6},{6,7},{7,8},{8,9},{9,10},{10,1... | collective-permute-start | bytes 49160 | tf_op jit(solution)/shard_map/ppermute | solution.py:283
  90.1 5.1 %collective-permute-done.30.refs_11_ = f32[8,512]{1,0:T(8,128)S(1)} collective-permute-done((f32[8,512]{1,0:T(8,128)S(1)}, f32[8,512]{1,0:T(8,128)S(1)}, u32[]{:S(2)}, u32[]{:S(2)}) %collective-permute-start.30) | collective-permute-done | bytes 16416 | tf_op jit(solution)/shard_map/ppermute | solution.py:282
  95.8 2.8 %shard_map.72 = (f32[19,16,512]{2,1,0:T(8,128)}, f32[16,512]{1,0:T(8,128)}) custom-call(bf16[4,19,16,512]{3,2,1,0:T(8,128)(2,1)} %refs_0_.7, f32[19,16,512]{2,1,0:T(8,128)} %get-tuple-element.40.refs_1_, s32[16,512]{1,0:T(8,128)} %refs_2_.7, s32[16,512]{1,0:T(8,128)} %refs_3_.7, f32[16,512]{1,0:T(8,128)} %refs_4_.7, ...), custom_call_target="tpu_custom_call", output_to_operand_aliasing={{1}: (13, {})} | custom-call | tf_op jit(solution)/shard_map/pallas_call | solution.py:257
  (109 shorter events, 13.1 us)
Async XLA Ops:
  2.3 10.6 %collective-permute-start = (f32[8,512]{1,0:T(8,128)}, f32[8,512]{1,0:T(8,128)S(1)}, u32[]{:S(2)}, u32[]{:S(2)}) collective-permute-start(f32[8,512]{1,0:T(8,128)} %get-tuple-element.24), channel_id=1, source_target_pairs={{0,224},{32,0},{64,32},{96,64},{128,96},{160,128},{192,160},{224,1... | collective-permute-start | bytes 49160 | tf_op jit(solution)/shard_map/ppermute | solution.py:276
  7.9 16.8 %collective-permute-start.2 = (f32[5,16,128]{2,1,0:T(8,128)}, f32[5,16,128]{2,1,0:T(8,128)S(1)}, u32[]{:S(2)}, u32[]{:S(2)}) collective-permute-start(f32[5,16,128]{2,1,0:T(8,128)} %get-tuple-element.26), channel_id=1, source_target_pairs={{0,31},{1,0},{2,1},{3,2},{4,3},{5,4},{6,5},{7,6},{8,7},{9,8},{10,9... | collective-permute-start | bytes 122888 | tf_op jit(solution)/shard_map/ppermute | solution.py:278
  8.9 15.9 %collective-permute-start.3 = (f32[5,16,128]{2,1,0:T(8,128)}, f32[5,16,128]{2,1,0:T(8,128)S(1)}, u32[]{:S(2)}, u32[]{:S(2)}) collective-permute-start(f32[5,16,128]{2,1,0:T(8,128)} %get-tuple-element.27), channel_id=1, source_target_pairs={{0,1},{1,2},{2,3},{3,4},{4,5},{5,6},{6,7},{7,8},{8,9},{9,10},{10,1... | collective-permute-start | bytes 122888 | tf_op jit(solution)/shard_map/ppermute | solution.py:279
  13.0 5.2 %collective-permute-start.5 = (f32[8,512]{1,0:T(8,128)S(1)}, f32[8,512]{1,0:T(8,128)S(1)}, u32[]{:S(2)}, u32[]{:S(2)}) collective-permute-start(f32[8,512]{1,0:T(8,128)S(1)} %collective-permute-done.refs_5_), channel_id=1, source_target_pairs={{0,1},{1,2},{2,3},{3,4},{4,5},{5,6},{6,7},{7,8},{8,9},{9,10},{10,1... | collective-permute-start | bytes 49160 | tf_op jit(solution)/shard_map/ppermute | solution.py:281
  13.1 6.6 %collective-permute-start.4 = (f32[8,512]{1,0:T(8,128)S(1)}, f32[8,512]{1,0:T(8,128)S(1)}, u32[]{:S(2)}, u32[]{:S(2)}) collective-permute-start(f32[8,512]{1,0:T(8,128)S(1)} %collective-permute-done.refs_5_), channel_id=1, source_target_pairs={{0,31},{1,0},{2,1},{3,2},{4,3},{5,4},{6,5},{7,6},{8,7},{9,8},{10,9... | collective-permute-start | bytes 49160 | tf_op jit(solution)/shard_map/ppermute | solution.py:280
  18.2 6.5 %collective-permute-start.6 = (f32[8,512]{1,0:T(8,128)S(1)}, f32[8,512]{1,0:T(8,128)S(1)}, u32[]{:S(2)}, u32[]{:S(2)}) collective-permute-start(f32[8,512]{1,0:T(8,128)S(1)} %collective-permute-done.1.refs_6_), channel_id=1, source_target_pairs={{0,31},{1,0},{2,1},{3,2},{4,3},{5,4},{6,5},{7,6},{8,7},{9,8},{10,9... | collective-permute-start | bytes 49160 | tf_op jit(solution)/shard_map/ppermute | solution.py:282
  28.8 7.9 %collective-permute-start.8 = (f32[8,512]{1,0:T(8,128)}, f32[8,512]{1,0:T(8,128)S(1)}, u32[]{:S(2)}, u32[]{:S(2)}) collective-permute-start(f32[8,512]{1,0:T(8,128)} %get-tuple-element.29), channel_id=1, source_target_pairs={{0,224},{32,0},{64,32},{96,64},{128,96},{160,128},{192,160},{224,1... | collective-permute-start | bytes 49160 | tf_op jit(solution)/shard_map/ppermute | solution.py:276
  31.7 16.8 %collective-permute-start.10 = (f32[5,16,128]{2,1,0:T(8,128)}, f32[5,16,128]{2,1,0:T(8,128)S(1)}, u32[]{:S(2)}, u32[]{:S(2)}) collective-permute-start(f32[5,16,128]{2,1,0:T(8,128)} %get-tuple-element.31), channel_id=1, source_target_pairs={{0,31},{1,0},{2,1},{3,2},{4,3},{5,4},{6,5},{7,6},{8,7},{9,8},{10,9... | collective-permute-start | bytes 122888 | tf_op jit(solution)/shard_map/ppermute | solution.py:278
  31.7 16.8 %collective-permute-start.11 = (f32[5,16,128]{2,1,0:T(8,128)}, f32[5,16,128]{2,1,0:T(8,128)S(1)}, u32[]{:S(2)}, u32[]{:S(2)}) collective-permute-start(f32[5,16,128]{2,1,0:T(8,128)} %get-tuple-element.32), channel_id=1, source_target_pairs={{0,1},{1,2},{2,3},{3,4},{4,5},{5,6},{6,7},{7,8},{8,9},{9,10},{10,1... | collective-permute-start | bytes 122888 | tf_op jit(solution)/shard_map/ppermute | solution.py:279
  36.8 5.2 %collective-permute-start.13 = (f32[8,512]{1,0:T(8,128)S(1)}, f32[8,512]{1,0:T(8,128)S(1)}, u32[]{:S(2)}, u32[]{:S(2)}) collective-permute-start(f32[8,512]{1,0:T(8,128)S(1)} %collective-permute-done.8.refs_5_), channel_id=1, source_target_pairs={{0,1},{1,2},{2,3},{3,4},{4,5},{5,6},{6,7},{7,8},{8,9},{9,10},{10,1... | collective-permute-start | bytes 49160 | tf_op jit(solution)/shard_map/ppermute | solution.py:281
  36.9 6.6 %collective-permute-start.12 = (f32[8,512]{1,0:T(8,128)S(1)}, f32[8,512]{1,0:T(8,128)S(1)}, u32[]{:S(2)}, u32[]{:S(2)}) collective-permute-start(f32[8,512]{1,0:T(8,128)S(1)} %collective-permute-done.8.refs_5_), channel_id=1, source_target_pairs={{0,31},{1,0},{2,1},{3,2},{4,3},{5,4},{6,5},{7,6},{8,7},{9,8},{10,9... | collective-permute-start | bytes 49160 | tf_op jit(solution)/shard_map/ppermute | solution.py:280
  42.0 6.5 %collective-permute-start.14 = (f32[8,512]{1,0:T(8,128)S(1)}, f32[8,512]{1,0:T(8,128)S(1)}, u32[]{:S(2)}, u32[]{:S(2)}) collective-permute-start(f32[8,512]{1,0:T(8,128)S(1)} %collective-permute-done.9.refs_6_), channel_id=1, source_target_pairs={{0,31},{1,0},{2,1},{3,2},{4,3},{5,4},{6,5},{7,6},{8,7},{9,8},{10,9... | collective-permute-start | bytes 49160 | tf_op jit(solution)/shard_map/ppermute | solution.py:282
  52.0 7.9 %collective-permute-start.16 = (f32[8,512]{1,0:T(8,128)}, f32[8,512]{1,0:T(8,128)S(1)}, u32[]{:S(2)}, u32[]{:S(2)}) collective-permute-start(f32[8,512]{1,0:T(8,128)} %get-tuple-element.35), channel_id=1, source_target_pairs={{0,224},{32,0},{64,32},{96,64},{128,96},{160,128},{192,160},{224,1... | collective-permute-start | bytes 49160 | tf_op jit(solution)/shard_map/ppermute | solution.py:276
  54.9 16.8 %collective-permute-start.18 = (f32[5,16,128]{2,1,0:T(8,128)}, f32[5,16,128]{2,1,0:T(8,128)S(1)}, u32[]{:S(2)}, u32[]{:S(2)}) collective-permute-start(f32[5,16,128]{2,1,0:T(8,128)} %get-tuple-element.37), channel_id=1, source_target_pairs={{0,31},{1,0},{2,1},{3,2},{4,3},{5,4},{6,5},{7,6},{8,7},{9,8},{10,9... | collective-permute-start | bytes 122888 | tf_op jit(solution)/shard_map/ppermute | solution.py:278
  54.9 16.8 %collective-permute-start.19 = (f32[5,16,128]{2,1,0:T(8,128)}, f32[5,16,128]{2,1,0:T(8,128)S(1)}, u32[]{:S(2)}, u32[]{:S(2)}) collective-permute-start(f32[5,16,128]{2,1,0:T(8,128)} %get-tuple-element.38), channel_id=1, source_target_pairs={{0,1},{1,2},{2,3},{3,4},{4,5},{5,6},{6,7},{7,8},{8,9},{9,10},{10,1... | collective-permute-start | bytes 122888 | tf_op jit(solution)/shard_map/ppermute | solution.py:279
  60.0 5.2 %collective-permute-start.21 = (f32[8,512]{1,0:T(8,128)S(1)}, f32[8,512]{1,0:T(8,128)S(1)}, u32[]{:S(2)}, u32[]{:S(2)}) collective-permute-start(f32[8,512]{1,0:T(8,128)S(1)} %collective-permute-done.16.refs_5_), channel_id=1, source_target_pairs={{0,1},{1,2},{2,3},{3,4},{4,5},{5,6},{6,7},{7,8},{8,9},{9,10},{10,1... | collective-permute-start | bytes 49160 | tf_op jit(solution)/shard_map/ppermute | solution.py:281
  60.1 6.6 %collective-permute-start.20 = (f32[8,512]{1,0:T(8,128)S(1)}, f32[8,512]{1,0:T(8,128)S(1)}, u32[]{:S(2)}, u32[]{:S(2)}) collective-permute-start(f32[8,512]{1,0:T(8,128)S(1)} %collective-permute-done.16.refs_5_), channel_id=1, source_target_pairs={{0,31},{1,0},{2,1},{3,2},{4,3},{5,4},{6,5},{7,6},{8,7},{9,8},{10,9... | collective-permute-start | bytes 49160 | tf_op jit(solution)/shard_map/ppermute | solution.py:280
  65.2 6.5 %collective-permute-start.22 = (f32[8,512]{1,0:T(8,128)S(1)}, f32[8,512]{1,0:T(8,128)S(1)}, u32[]{:S(2)}, u32[]{:S(2)}) collective-permute-start(f32[8,512]{1,0:T(8,128)S(1)} %collective-permute-done.17.refs_6_), channel_id=1, source_target_pairs={{0,31},{1,0},{2,1},{3,2},{4,3},{5,4},{6,5},{7,6},{8,7},{9,8},{10,9... | collective-permute-start | bytes 49160 | tf_op jit(solution)/shard_map/ppermute | solution.py:282
  75.2 7.9 %collective-permute-start.24 = (f32[8,512]{1,0:T(8,128)}, f32[8,512]{1,0:T(8,128)S(1)}, u32[]{:S(2)}, u32[]{:S(2)}) collective-permute-start(f32[8,512]{1,0:T(8,128)} %get-tuple-element.41), channel_id=1, source_target_pairs={{0,224},{32,0},{64,32},{96,64},{128,96},{160,128},{192,160},{224,1... | collective-permute-start | bytes 49160 | tf_op jit(solution)/shard_map/ppermute | solution.py:276
  78.1 17.0 %collective-permute-start.26 = (f32[5,16,128]{2,1,0:T(8,128)}, f32[5,16,128]{2,1,0:T(8,128)S(1)}, u32[]{:S(2)}, u32[]{:S(2)}) collective-permute-start(f32[5,16,128]{2,1,0:T(8,128)} %get-tuple-element.43), channel_id=1, source_target_pairs={{0,31},{1,0},{2,1},{3,2},{4,3},{5,4},{6,5},{7,6},{8,7},{9,8},{10,9... | collective-permute-start | bytes 122888 | tf_op jit(solution)/shard_map/ppermute | solution.py:278
  78.1 17.0 %collective-permute-start.27 = (f32[5,16,128]{2,1,0:T(8,128)}, f32[5,16,128]{2,1,0:T(8,128)S(1)}, u32[]{:S(2)}, u32[]{:S(2)}) collective-permute-start(f32[5,16,128]{2,1,0:T(8,128)} %get-tuple-element.44), channel_id=1, source_target_pairs={{0,1},{1,2},{2,3},{3,4},{4,5},{5,6},{6,7},{7,8},{8,9},{9,10},{10,1... | collective-permute-start | bytes 122888 | tf_op jit(solution)/shard_map/ppermute | solution.py:279
  83.2 5.5 %collective-permute-start.29 = (f32[8,512]{1,0:T(8,128)S(1)}, f32[8,512]{1,0:T(8,128)S(1)}, u32[]{:S(2)}, u32[]{:S(2)}) collective-permute-start(f32[8,512]{1,0:T(8,128)S(1)} %collective-permute-done.24.refs_5_), channel_id=1, source_target_pairs={{0,1},{1,2},{2,3},{3,4},{4,5},{5,6},{6,7},{7,8},{8,9},{9,10},{10,1... | collective-permute-start | bytes 49160 | tf_op jit(solution)/shard_map/ppermute | solution.py:281
  83.5 6.6 %collective-permute-start.28 = (f32[8,512]{1,0:T(8,128)S(1)}, f32[8,512]{1,0:T(8,128)S(1)}, u32[]{:S(2)}, u32[]{:S(2)}) collective-permute-start(f32[8,512]{1,0:T(8,128)S(1)} %collective-permute-done.24.refs_5_), channel_id=1, source_target_pairs={{0,31},{1,0},{2,1},{3,2},{4,3},{5,4},{6,5},{7,6},{8,7},{9,8},{10,9... | collective-permute-start | bytes 49160 | tf_op jit(solution)/shard_map/ppermute | solution.py:280
  88.7 6.5 %collective-permute-start.30 = (f32[8,512]{1,0:T(8,128)S(1)}, f32[8,512]{1,0:T(8,128)S(1)}, u32[]{:S(2)}, u32[]{:S(2)}) collective-permute-start(f32[8,512]{1,0:T(8,128)S(1)} %collective-permute-done.25.refs_6_), channel_id=1, source_target_pairs={{0,31},{1,0},{2,1},{3,2},{4,3},{5,4},{6,5},{7,6},{8,7},{9,8},{10,9... | collective-permute-start | bytes 49160 | tf_op jit(solution)/shard_map/ppermute | solution.py:282
  (40 other events, 179.9 us)
